TPU v7x, 32 devices: a whole 2x2x4 slice. The times are simulated.
32 devices in a mesh: fsdp: 8 (over y, x, core), dp: 4 (over z).
Axes of the slice: x: 2, y: 2, z: 4, core: 2. Of those that a mesh axis runs over, the one named last changes fastest.
Arguments:
- tokens: bfloat16 [12288, 8192], P(('fsdp', 'dp')), may hold values from -6 to 6
- output_gradient: bfloat16 [12288, 1024], P(('fsdp', 'dp')), may hold values from -6 to 6
- frozen_value_weight: bfloat16 [8192, 1024], P('fsdp'), may hold values from -0.0625 to 0.0625
- adapter_down_maps: bfloat16 [32, 16, 8192], P(('fsdp', 'dp')), may hold values from -0.0625 to 0.0625
- adapter_up_maps: bfloat16 [32, 16, 1024], P(('fsdp', 'dp')), may hold values from -1.5 to 1.5
- block_tenant_ids: int32 [96], P(('fsdp', 'dp')), may hold values from 0 to 31, as said below
- block_live_rows: int32 [96], P(('fsdp', 'dp')), may hold values from 33 to 128, as said below
- tenant_owner_slot: int32 [32], replicated, may hold values from 0 to 31, as said below
Outputs:
- output: bfloat16 [12288, 1024], P(('fsdp', 'dp'))
- token_gradient: bfloat16 [12288, 8192], P(('fsdp', 'dp'))
- grad_down: bfloat16 [32, 16, 8192], P(('fsdp', 'dp'))
- grad_up: bfloat16 [32, 16, 1024], P(('fsdp', 'dp'))
Inputs may be any that keep to these rules, and one draw needn't show every extreme that they name: `block_tenant_ids`: A block held by a device whose index along dp is d names a tenant t with tenant_owner_slot[t] mod (size of dp) = d; tenant_owner_slot is a permutation. `block_live_rows`: the first block of every device is full. `tenant_owner_slot`: each slot is named once.
All inputs are finite; a program needn't handle non-finite values.
Results may differ from a plain program's by a relative error of at most 0.01.
Values may be sent and summed in bfloat16 or wider, within the bound.
No kernel may reach another device: no remote copies, remote signals or barrier semaphores. Data moves between devices by JAX's collectives and lax.ppermute only.
A program may use at most 192 MiB of HBM per device.

v0:
```python
import jax
import jax.numpy as jnp
from jax import lax
from jax.sharding import PartitionSpec as P

ADAPTER_SCALE = 2.0


def on_device(
    tokens,
    output_gradient,
    frozen_value_weight,
    adapter_down_maps,
    adapter_up_maps,
    block_tenant_ids,
    block_live_rows,
    tenant_owner_slot,
):
    tok_rows = tokens.shape[0]
    model_width_size = tokens.shape[1]
    value_width_size = output_gradient.shape[1]
    adapter_rank_size = adapter_down_maps.shape[1]
    number_of_blocks = block_tenant_ids.shape[0]
    block_length = tok_rows // number_of_blocks
    groups = lax.axis_size("dp")
    members = lax.axis_size("fsdp")
    tenant_ids = jnp.arange(tenant_owner_slot.shape[0], dtype=jnp.int32)
    slot_ids = jnp.sum(
        jnp.where(block_tenant_ids[:, None] == tenant_ids[None, :], tenant_owner_slot[None, :], 0),
        axis=1,
    )
    member_ids = slot_ids // groups
    live_rows = (jnp.arange(block_length)[None, :] < block_live_rows[:, None]).astype(jnp.float32)
    live_column = live_rows[:, :, None]
    down_all, up_all = (
        lax.all_gather(adapter_down_maps, "fsdp", axis=0, tiled=True),
        lax.all_gather(adapter_up_maps, "fsdp", axis=0, tiled=True),
    )
    onehot = (member_ids[:, None] == jnp.arange(members)[None, :]).astype(jnp.bfloat16)
    down_block = jnp.dot(onehot, down_all.reshape(members, -1), preferred_element_type=jnp.float32)
    down_block = down_block.astype(jnp.bfloat16).reshape(
        number_of_blocks, adapter_rank_size, model_width_size
    )
    up_block = jnp.dot(onehot, up_all.reshape(members, -1), preferred_element_type=jnp.float32)
    up_block = up_block.astype(jnp.bfloat16).reshape(
        number_of_blocks, adapter_rank_size, value_width_size
    )
    token_blocks = tokens.reshape(number_of_blocks, block_length, model_width_size)
    cot_blocks = output_gradient.reshape(number_of_blocks, block_length, value_width_size)
    low_rank_state = (
        jnp.einsum("cvj,coj->cvo", token_blocks, down_block, preferred_element_type=jnp.float32)
        * live_column
    ).astype(jnp.bfloat16)
    low_rank_gradient = (
        ADAPTER_SCALE
        * jnp.einsum("btv,bkv->btk", cot_blocks, up_block, preferred_element_type=jnp.float32)
        * live_column
    ).astype(jnp.bfloat16)
    adapter_output = jnp.einsum(
        "znr,zrm->znm", low_rank_state, up_block, preferred_element_type=jnp.float32
    )
    adapter_backward = jnp.einsum(
        "uio,uof->uif", low_rank_gradient, down_block, preferred_element_type=jnp.float32
    )
    weight_piece = lax.all_gather(frozen_value_weight, "fsdp", axis=0, tiled=True)
    output_total = jnp.dot(tokens, weight_piece, preferred_element_type=jnp.float32)
    backward_piece = lax.dot_general(
        output_gradient, weight_piece, (((1,), (1,)), ((), ())), preferred_element_type=jnp.float32
    )
    output = live_column * (
        output_total.reshape(number_of_blocks, block_length, value_width_size)
        + ADAPTER_SCALE * adapter_output
    )
    output = output.astype(jnp.bfloat16).reshape(tok_rows, value_width_size)
    token_gradient = live_column * (
        backward_piece.reshape(number_of_blocks, block_length, model_width_size) + adapter_backward
    )
    token_gradient = token_gradient.astype(jnp.bfloat16).reshape(tok_rows, model_width_size)
    partial_down = jnp.einsum(
        "vio,vih->voh", low_rank_gradient, token_blocks, preferred_element_type=jnp.float32
    )
    partial_up = ADAPTER_SCALE * jnp.einsum(
        "btk,btv->bkv", low_rank_state, cot_blocks, preferred_element_type=jnp.float32
    )
    member_range = jnp.arange(members, dtype=jnp.int32)
    table_down = jnp.zeros((members, adapter_rank_size, model_width_size), jnp.float32)
    table_up = jnp.zeros((members, adapter_rank_size, value_width_size), jnp.float32)
    for block_num in range(number_of_blocks):
        picked = (member_range == member_ids[block_num]).astype(jnp.float32)[:, None, None]
        table_down = table_down + picked * partial_down[block_num][None]
        table_up = table_up + picked * partial_up[block_num][None]
    term_down = table_down.astype(jnp.bfloat16)
    term_up = table_up.astype(jnp.bfloat16)
    sum_down, sum_up = (
        lax.psum_scatter(
            term_down.astype(jnp.float32).astype(jnp.bfloat16),
            "fsdp",
            scatter_dimension=0,
            tiled=True,
        ).astype(jnp.float32),
        lax.psum_scatter(
            term_up.astype(jnp.float32).astype(jnp.bfloat16),
            "fsdp",
            scatter_dimension=0,
            tiled=True,
        ).astype(jnp.float32),
    )
    return (output, token_gradient, sum_down.astype(jnp.bfloat16), sum_up.astype(jnp.bfloat16))


def solution(mesh):
    placed = (
        P(("fsdp", "dp"), None),
        P(("fsdp", "dp"), None),
        P("fsdp", None),
        P(("fsdp", "dp"), None, None),
        P(("fsdp", "dp"), None, None),
        P(("fsdp", "dp")),
        P(("fsdp", "dp")),
        P(),
    )
    return jax.shard_map(
        on_device,
        mesh=mesh,
        in_specs=placed,
        out_specs=(
            P(("fsdp", "dp"), None),
            P(("fsdp", "dp"), None),
            P(("fsdp", "dp"), None, None),
            P(("fsdp", "dp"), None, None),
        ),
        check_vma=False,
    )
```

profile of v0, /device:TPU:0, one launch (start us, length us, event | category | flops | bytes accessed | tf_op | source)
XLA Modules:
  0.0 221.4 jit_solution(15387211955821967845)
XLA Ops:
  7.2 0.0 all-gather.5.cloned.1.call-start
  7.2 0.7 all-gather.5.cloned.1.call-update
  7.9 0.0 all-gather.3.cloned.1.call-start
  8.0 0.7 all-gather.3.cloned.1.call-update
  8.7 0.0 reduce-scatter.3.cloned.1.call-start
  8.7 11.0 %all_gather.11 = bf16[8,16,1024]{2,1,0:T(8,128)(2,1)S(1)} all-gather(bf16[1,16,1024]{2,1,0:T(8,128)(2,1)} %param.12), channel_id=1, replica_groups=mesh['fsdp'=8,'dp'=4] {'fsdp'}, dimensions={0}, use_global_device_ids=true | all-gather | bytes 294912 | tf_op jit(solution)/shard_map/all_gather | solution.py:37
  19.7 0.1 copy.14
  19.8 0.9 select_reduce_fusion
  20.7 0.6 fusion.14
  21.3 0.6 compare_convert_fusion.2
  22.0 1.3 compare_convert_fusion
  23.3 0.7 fusion.10
  24.0 0.3 convolution_convert_fusion.1
  24.3 0.3 fusion.1
  24.6 3.7 %fusion.17 = f32[3,16,8192]{2,1,0:T(8,128)S(1)} fusion(bf16[3,16,128]{2,1,0:T(8,128)(2,1)S(1)} %fusion.1, bf16[3,128,8192]{2,1,0:T(8,128)(2,1)} %bitcast.53), kind=kOutput, calls=%fused_computation.43 | convolution fusion | flops 100663296 | bytes 7876608 | tf_op jit(solution)/shard_map/vio,vih->voh/dot_general | solution.py:79
  28.3 0.1 slice_bitcast_fusion.2
  28.4 2.2 add_convert_fusion
  30.6 0.2 reduce-scatter.5.cloned.1.call-start
  30.8 0.1 fusion.11
  30.9 9.6 %all-gather.5.cloned.1.call-done = bf16[8,16,8192]{2,1,0:T(8,128)(2,1)} async-done(((bf16[1,16,8192]{2,1,0:T(8,128)(2,1)}), bf16[8,16,8192]{2,1,0:T(8,128)(2,1)}) %all-gather.5.cloned.1.call-update) | async-done | bytes 2097168 | tf_op jit(solution)/shard_map/all_gather | solution.py:36
  40.5 2.7 %copy.12 = bf16[1,8,16,8192]{3,1,2,0:T(8,128)(2,1)S(1)} copy(bf16[1,8,16,8192]{3,2,1,0:T(8,128)(2,1)} %bitcast.60) | data formatting | bytes 4194304
  43.3 0.8 convolution_convert_fusion
  44.0 4.5 %fusion = bf16[3,16,128]{2,1,0:T(8,128)(2,1)S(1)} fusion(bf16[3,128,8192]{2,1,0:T(8,128)(2,1)} %bitcast.54, bf16[1,3,16,8192]{3,1,2,0:T(4,128)(2,1)S(1)} %bitcast.57, f32[3,128]{1,0:T(4,128)S(1)} %fusion.11), kind=kOutput, calls=%fused_computation.8 | convolution fusion | flops 100675584 | bytes 7091712 | tf_op jit(solution)/shard_map/cvj,coj->cvo/dot_general | solution.py:51
  48.6 0.2 convolution_multiply_fusion
  48.8 0.9 add_convert_fusion.1
  49.7 82.6 %all-gather.3.cloned.1.call-done = bf16[8192,1024]{1,0:T(8,128)(2,1)} async-done(((bf16[1024,1024]{1,0:T(8,128)(2,1)}), bf16[8192,1024]{1,0:T(8,128)(2,1)}) %all-gather.3.cloned.1.call-update) | async-done | bytes 16777232 | tf_op jit(solution)/shard_map/all_gather | solution.py:65
  132.3 12.1 %fusion.15 = f32[384,1024]{1,0:T(8,128)S(1)} fusion(bf16[384,8192]{1,0:T(8,128)(2,1)} %param.8, bf16[8192,1024]{1,0:T(8,128)(2,1)} %all-gather.3.cloned.1.call-done), kind=kOutput, calls=%fused_computation.41 | convolution fusion | flops 6442450944 | bytes 24641536 | tf_op jit(solution)/shard_map/dot_general | solution.py:66
  144.4 13.4 %fusion.16 = f32[384,8192]{1,0:T(8,128)} fusion(bf16[384,1024]{1,0:T(8,128)(2,1)S(1)} %copy-done, bf16[8192,1024]{1,0:T(8,128)(2,1)} %all-gather.3.cloned.1.call-done), kind=kOutput, calls=%fused_computation.42 | convolution fusion | flops 6442450944 | bytes 30146560 | tf_op jit(solution)/shard_map/dot_general | solution.py:67
  157.8 9.2 %multiply_convert_fusion = bf16[3,128,8192]{2,1,0:T(8,128)(2,1)} fusion(f32[3,128,8192]{2,1,0:T(8,128)} %bitcast.55, bf16[3,16,128]{2,1,0:T(8,128)(2,1)S(1)} %fusion.1, f32[3,128]{1,0:T(4,128)S(1)} %fusion.11, bf16[1,3,16,8192]{3,1,2,0:T(4,128)(2,1)S(1)} %bitcast.58), kind=kOutput, calls=%fused_computation.2 | convolution fusion | flops 110100480 | bytes 19674624 | tf_op jit(solution)/shard_map/uio,uof->uif/dot_general | solution.py:62
  167.0 1.3 multiply_convert_fusion.1
  168.3 9.2 %reduce-scatter.3.cloned.1.call-done = bf16[1,16,8192]{2,1,0:T(8,128)(2,1)} async-done(((bf16[8,16,8192]{2,1,0:T(8,128)(2,1)}), bf16[1,16,8192]{2,1,0:T(8,128)(2,1)}) %reduce-scatter.3.cloned.1.call-update) | async-done | bytes 262160 | tf_op jit(solution)/shard_map/reduce_scatter | solution.py:95
  177.4 37.4 %reduce-scatter.5.cloned.1.call-done = bf16[1,16,1024]{2,1,0:T(8,128)(2,1)} async-done(((bf16[8,16,1024]{2,1,0:T(8,128)(2,1)}), bf16[1,16,1024]{2,1,0:T(8,128)(2,1)}) %reduce-scatter.5.cloned.1.call-update) | async-done | bytes 32784 | tf_op jit(solution)/shard_map/reduce_scatter | solution.py:101
  (8 shorter events, 0.1 us)
Async XLA Ops:
  7.2 17.1 %copy-start = (bf16[384,1024]{1,0:T(8,128)(2,1)S(1)}, bf16[384,1024]{1,0:T(8,128)(2,1)}, u32[]{:S(2)}) copy-start(bf16[384,1024]{1,0:T(8,128)(2,1)} %param.9) | copy-start | bytes 2359300
  7.2 33.4 %all-gather.5.cloned.1.call-start = ((), (), s32[]{:S(2)}) async-start(), calls=%async_computation.3 | async-start | bytes 2359296 | tf_op jit(solution)/shard_map/all_gather | solution.py:36
  7.9 124.4 %all-gather.3.cloned.1.call-start = ((), (), s32[]{:S(2)}) async-start(), calls=%async_computation.2 | async-start | bytes 18874368 | tf_op jit(solution)/shard_map/all_gather | solution.py:65
  8.7 168.8 %reduce-scatter.3.cloned.1.call-start = ((), (), s32[]{:S(2)}) async-start(), calls=%async_computation.4 | async-start | bytes 2359296 | tf_op jit(solution)/shard_map/reduce_scatter | solution.py:95
  28.3 2.5 %copy-start.1 = (s32[3]{0:T(128)S(1)}, s32[3]{0:T(128)}, u32[]{:S(2)}) copy-start(s32[3]{0:T(128)} %param.14) | copy-start | bytes 40
  30.6 184.2 %reduce-scatter.5.cloned.1.call-start = ((), (), s32[]{:S(2)}) async-start(), calls=%async_computation.5 | async-start | bytes 294912 | tf_op jit(solution)/shard_map/reduce_scatter | solution.py:101
Sparse Core Ops, SparseCore 0:
  9.9 30.5 all-gather.4
  42.4 89.8 all-gather.2
  136.2 41.2 reduce-scatter.2
  181.2 33.5 reduce-scatter.4
where the time goes:
time: 222 us; the launch traced here: 221 us
  waiting for transfers between devices  140 us (63%)
  matrix products  45.8 us (21%)
  between operations  13.8 us (6%)
  blocking collectives  11 us (5%)
  other arithmetic  6.64 us (3%)
  local copies, waits for them, and re-layouts  3.62 us (2%)
    all_gather x1, waiting for transfers between devices, on_device(): lax.all_gather(frozen_value_weight, 'fsdp', axis=0, tiled=True)  82.6 us
    reduce_scatter x1, waiting for transfers between devices, on_device(): lax.psum_scatter(term_up.astype(jnp.float32).astype(jnp.bfloat16), 'fsdp'...  37.4 us
    dot_general x1, matrix products, on_device(): lax.dot_general(output_gradient, weight_piece, (((1,), (1,)), ((), ())),...  13.4 us
    dot_general x1, matrix products, on_device(): jnp.dot(tokens, weight_piece, preferred_element_type=jnp.float32)  12.1 us
    all_gather x1, blocking collectives, on_device(): lax.all_gather(adapter_up_maps, 'fsdp', axis=0, tiled=True)  11 us
    all_gather x1, waiting for transfers between devices, on_device(): lax.all_gather(adapter_down_maps, 'fsdp', axis=0, tiled=True)  9.62 us
    dot_general x1, matrix products, on_device(): jnp.einsum('uio,uof->uif', low_rank_gradient, down_block, preferred_eleme...  9.17 us
    reduce_scatter x1, waiting for transfers between devices, on_device(): lax.psum_scatter(term_down.astype(jnp.float32).astype(jnp.bfloat16), 'fsd...  9.16 us
  transfers between devices with their start and end apart: 4, of which 4 were waited for; matrix products, arithmetic and copies ran while one was open for 25% of the time, Pallas kernels for 0%

commit v1 on v0

--- a/solution.py
+++ b/solution.py
@@ -62,7 +62,34 @@
     adapter_backward = jnp.einsum(
         "uio,uof->uif", low_rank_gradient, down_block, preferred_element_type=jnp.float32
     )
-    weight_piece = lax.all_gather(frozen_value_weight, "fsdp", axis=0, tiled=True)
+    block_out, far_arr, row_out = (
+        lax.axis_size("fsdp"),
+        lax.axis_index("fsdp"),
+        frozen_value_weight.shape[0],
+    )
+    ledger = [(t, (t + 1) % block_out) for t in range(block_out)]
+    fields = [(t, (t - 1) % block_out) for t in range(block_out)]
+    weight_piece = jnp.zeros(
+        (*frozen_value_weight.shape[:0], block_out * row_out, *frozen_value_weight.shape[1:]),
+        frozen_value_weight.dtype,
+    )
+    parts_out = r_now = frozen_value_weight
+    z2 = block_out // 2
+    tick = 1
+    weight_piece = lax.dynamic_update_slice_in_dim(
+        weight_piece, frozen_value_weight, far_arr * row_out, axis=0
+    )
+    while tick < z2 + 1:
+        parts_out = lax.ppermute(parts_out, "fsdp", ledger)
+        weight_piece = lax.dynamic_update_slice_in_dim(
+            weight_piece, parts_out, (far_arr - tick) % block_out * row_out, axis=0
+        )
+        if tick < block_out - z2:
+            r_now = lax.ppermute(r_now, "fsdp", fields)
+            weight_piece = lax.dynamic_update_slice_in_dim(
+                weight_piece, r_now, (far_arr + tick) % block_out * row_out, axis=0
+            )
+        tick = tick + 1
     output_total = jnp.dot(tokens, weight_piece, preferred_element_type=jnp.float32)
     backward_piece = lax.dot_general(
         output_gradient, weight_piece, (((1,), (1,)), ((), ())), preferred_element_type=jnp.float32

time: 222 us -> 262 us (1.18)
  waiting for transfers between devices: 140 us -> 82.8 us
  blocking collectives: 11 us -> 58.2 us
  local copies, waits for them, and re-layouts: 3.62 us -> 31.5 us
  other arithmetic: 6.64 us -> 16.5 us
  starting transfers between devices: 0.34 us -> 9 us
  matrix products: 45.8 us -> 49.1 us
    ppermute x0 -> x7, waiting for transfers between devices: none -> 82.7 us  [the longest x4 70.9 us: on_device(): parts_out = lax.ppermute(parts_out, 'fsdp', ledger)]
    all_gather x1 -> x0, waiting for transfers between devices: 82.6 us -> none  [on_device(): lax.all_gather(frozen_value_weight, 'fsdp', axis=0, tiled=True)]
    all_gather x1, blocking collectives: 11 us -> 58.2 us  [on_device(): lax.all_gather(adapter_up_maps, 'fsdp', axis=0, tiled=True)]
    reduce_scatter x1, waiting for transfers between devices: 37.4 us -> 0.01 us  [on_device(): lax.psum_scatter(term_up.astype(jnp.float32).astype(jnp.bfloat16), 'fsdp'...]
    dynamic_update_slice x0 -> x8, local copies, waits for them, and re-layouts: none -> 21.9 us  [the longest x4 11 us: on_device(): lax.dynamic_update_slice_in_dim(weight_piece, parts_out, (far_arr - tick)...]
    dot_general x1, matrix products: 13.4 us -> 24.6 us  [on_device(): lax.dot_general(output_gradient, weight_piece, (((1,), (1,)), ((), ())),...]
    convert_element_type x0 -> x2, other arithmetic: none -> 9.82 us  [the longest x1 8.69 us: on_device(): token_gradient.astype(jnp.bfloat16).reshape(tok_rows, model_width_size)]
    all_gather x1, waiting for transfers between devices: 9.62 us -> 0.01 us  [on_device(): lax.all_gather(adapter_down_maps, 'fsdp', axis=0, tiled=True)]
  transfers between devices with their start and end apart: 4 -> 10, of which waited for: 4 -> 4; matrix products, arithmetic and copies ran while one was open for 25% -> 37% of each run, Pallas kernels for 0% -> 0%
where the time goes in v1:
time: 262 us; the launch traced here: 261 us
  waiting for transfers between devices  82.8 us (32%)
  blocking collectives  58.2 us (22%)
  matrix products  49.1 us (19%)
  local copies, waits for them, and re-layouts  31.5 us (12%)
  other arithmetic  16.5 us (6%)
  between operations  13.9 us (5%)
  starting transfers between devices  9 us (3%)
    ppermute x4, waiting for transfers between devices, on_device(): parts_out = lax.ppermute(parts_out, 'fsdp', ledger)  70.9 us
    all_gather x1, blocking collectives, on_device(): lax.all_gather(adapter_up_maps, 'fsdp', axis=0, tiled=True)  58.2 us
    dot_general x1, matrix products, on_device(): lax.dot_general(output_gradient, weight_piece, (((1,), (1,)), ((), ())),...  24.6 us
    ppermute x3, waiting for transfers between devices, on_device(): r_now = lax.ppermute(r_now, 'fsdp', fields)  11.9 us
    dynamic_update_slice x4, local copies, waits for them, and re-layouts, on_device(): lax.dynamic_update_slice_in_dim(weight_piece, parts_out, (far_arr - tick)...  11 us
    dot_general x1, matrix products, on_device(): jnp.dot(tokens, weight_piece, preferred_element_type=jnp.float32)  10.5 us
    dynamic_update_slice x3, local copies, waits for them, and re-layouts, on_device(): lax.dynamic_update_slice_in_dim(weight_piece, r_now, (far_arr + tick) % b...  9.34 us
    convert_element_type x1, other arithmetic, on_device(): token_gradient.astype(jnp.bfloat16).reshape(tok_rows, model_width_size)  8.69 us
  transfers between devices with their start and end apart: 10, of which 4 were waited for; matrix products, arithmetic and copies ran while one was open for 37% of the time, Pallas kernels for 0%

profile of v1, /device:TPU:0, one launch (start us, length us, event | category | flops | bytes accessed | tf_op | source)
XLA Modules:
  0.0 261.1 jit_solution(792765522471908547)
XLA Ops:
  7.7 2.9 %collective-permute-start.1 = (bf16[1024,1024]{1,0:T(8,128)(2,1)}, bf16[1024,1024]{1,0:T(8,128)(2,1)}, u32[]{:S(2)}, u32[]{:S(2)}) collective-permute-start(bf16[1024,1024]{1,0:T(8,128)(2,1)} %param.10), channel_id=1, source_target_pairs={{0,28},{4,0},{8,4},{12,8},{16,12},{20,16},{24,20},{28,24},{1,29},{... | collective-permute-start | bytes 6291464 | tf_op jit(solution)/shard_map/ppermute | solution.py:88
  10.8 0.9 select_reduce_fusion
  11.6 58.2 %all_gather.7 = bf16[8,16,1024]{2,1,0:T(8,128)(2,1)S(1)} all-gather(bf16[1,16,1024]{2,1,0:T(8,128)(2,1)} %param.12), channel_id=1, replica_groups=mesh['fsdp'=8,'dp'=4] {'fsdp'}, dimensions={0}, use_global_device_ids=true | all-gather | bytes 294912 | tf_op jit(solution)/shard_map/all_gather | solution.py:37
  71.3 3.7 %fusion.18 = f32[3,16,8192]{2,1,0:T(8,128)S(1)} fusion(bf16[3,16,128]{2,1,0:T(8,128)(2,1)S(1)} %fusion.1, bf16[3,128,8192]{2,1,0:T(8,128)(2,1)} %bitcast.57), kind=kOutput, calls=%fused_computation.52 | convolution fusion | flops 100663296 | bytes 7876608 | tf_op jit(solution)/shard_map/vio,vih->voh/dot_general | solution.py:106
  76.3 1.3 compare_convert_fusion
  78.2 2.3 collective-permute-start.3
  80.5 2.2 add_convert_fusion
  82.7 51.2 %collective-permute-done.2 = bf16[1024,1024]{1,0:T(8,128)(2,1)} collective-permute-done((bf16[1024,1024]{1,0:T(8,128)(2,1)S(1)}, bf16[1024,1024]{1,0:T(8,128)(2,1)}, u32[]{:S(2)}, u32[]{:S(2)}) %collective-permute-start.2) | collective-permute-done | bytes 2097184 | tf_op jit(solution)/shard_map/ppermute | solution.py:83
  133.9 6.0 %broadcast_in_dim.14 = bf16[8192,1024]{1,0:T(8,128)(2,1)} broadcast(bf16[]{:T(256)} %constant.64.clone.1), dimensions={} | broadcast | bytes 16777218 | tf_op jit(solution)/shard_map/broadcast_in_dim | solution.py:72
  139.9 1.5 constant_dynamic-update-slice_fusion.7
  141.5 1.5 constant_dynamic-update-slice_fusion.6
  143.0 3.1 %constant_dynamic-update-slice_fusion.5 = bf16[8192,1024]{1,0:T(8,128)(2,1)} fusion(bf16[8192,1024]{1,0:T(8,128)(2,1)} %constant_dynamic-update-slice_fusion.6, bf16[1024,1024]{1,0:T(8,128)(2,1)} %collective-permute-done.1, s32[]{:T(128)S(6)} %select_n.72), kind=kLoop, calls=%fused_computation.35 | loop fusion | bytes 4194308 | tf_op jit(solution)/shard_map/dynamic_update_slice | solution.py:89
  146.1 2.8 %copy.12 = bf16[1,8,16,8192]{3,1,2,0:T(8,128)(2,1)S(1)} copy(bf16[1,8,16,8192]{3,2,1,0:T(8,128)(2,1)} %bitcast.66) | data formatting | bytes 4194304
  148.8 0.8 convolution_convert_fusion
  149.6 2.7 %collective-permute-start.5 = (bf16[1024,1024]{1,0:T(8,128)(2,1)}, bf16[1024,1024]{1,0:T(8,128)(2,1)}, u32[]{:S(2)}, u32[]{:S(2)}) collective-permute-start(bf16[1024,1024]{1,0:T(8,128)(2,1)} %collective-permute-done.3), channel_id=1, source_target_pairs={{0,28},{4,0},{8,4},{12,8},{16,12},{20,16},{24,20},{28,24},{1,29},{... | collective-permute-start | bytes 6291464 | tf_op jit(solution)/shard_map/ppermute | solution.py:88
  152.3 5.1 %fusion = bf16[3,16,128]{2,1,0:T(8,128)(2,1)} fusion(bf16[3,128,8192]{2,1,0:T(8,128)(2,1)} %bitcast.58, bf16[1,3,16,8192]{3,1,2,0:T(4,128)(2,1)S(1)} %bitcast.63, f32[3,128]{1,0:T(4,128)S(1)} %fusion.13), kind=kOutput, calls=%fused_computation.8 | convolution fusion | flops 100675584 | bytes 7091712 | tf_op jit(solution)/shard_map/cvj,coj->cvo/dot_general | solution.py:51
  157.4 12.6 %collective-permute-done.4 = bf16[1024,1024]{1,0:T(8,128)(2,1)} collective-permute-done((bf16[1024,1024]{1,0:T(8,128)(2,1)}, bf16[1024,1024]{1,0:T(8,128)(2,1)}, u32[]{:S(2)}, u32[]{:S(2)}) %collective-permute-start.4) | collective-permute-done | bytes 2097184 | tf_op jit(solution)/shard_map/ppermute | solution.py:83
  170.0 0.9 convolution_multiply_fusion
  171.0 0.9 add_convert_fusion.1
  171.9 1.1 fusion.8
  173.0 1.8 fusion.2
  174.8 3.1 %constant_dynamic-update-slice_fusion.4 = bf16[8192,1024]{1,0:T(8,128)(2,1)} fusion(bf16[8192,1024]{1,0:T(8,128)(2,1)} %constant_dynamic-update-slice_fusion.5, bf16[1024,1024]{1,0:T(8,128)(2,1)} %collective-permute-done.2, s32[]{:T(128)S(6)} %select_n.74), kind=kLoop, calls=%fused_computation.34 | loop fusion | bytes 4194308 | tf_op jit(solution)/shard_map/dynamic_update_slice | solution.py:84
  177.9 3.1 %constant_dynamic-update-slice_fusion.3 = bf16[8192,1024]{1,0:T(8,128)(2,1)} fusion(bf16[8192,1024]{1,0:T(8,128)(2,1)} %constant_dynamic-update-slice_fusion.4, bf16[1024,1024]{1,0:T(8,128)(2,1)} %collective-permute-done.3, s32[]{:T(128)S(6)} %select_n.76), kind=kLoop, calls=%fused_computation.33 | loop fusion | bytes 4194308 | tf_op jit(solution)/shard_map/dynamic_update_slice | solution.py:89
  181.1 3.1 %constant_dynamic-update-slice_fusion.2 = bf16[8192,1024]{1,0:T(8,128)(2,1)} fusion(bf16[8192,1024]{1,0:T(8,128)(2,1)} %constant_dynamic-update-slice_fusion.3, bf16[1024,1024]{1,0:T(8,128)(2,1)} %collective-permute-done.4, s32[]{:T(128)S(6)} %select_n.78), kind=kLoop, calls=%fused_computation.32 | loop fusion | bytes 4194308 | tf_op jit(solution)/shard_map/dynamic_update_slice | solution.py:84
  184.2 11.8 %collective-permute-done.5 = bf16[1024,1024]{1,0:T(8,128)(2,1)} collective-permute-done((bf16[1024,1024]{1,0:T(8,128)(2,1)}, bf16[1024,1024]{1,0:T(8,128)(2,1)}, u32[]{:S(2)}, u32[]{:S(2)}) %collective-permute-start.5) | collective-permute-done | bytes 2097184 | tf_op jit(solution)/shard_map/ppermute | solution.py:88
  196.1 3.1 %constant_dynamic-update-slice_fusion.1 = bf16[8192,1024]{1,0:T(8,128)(2,1)} fusion(bf16[8192,1024]{1,0:T(8,128)(2,1)} %constant_dynamic-update-slice_fusion.2, bf16[1024,1024]{1,0:T(8,128)(2,1)} %collective-permute-done.5, s32[]{:T(128)S(6)} %select_n.80), kind=kLoop, calls=%fused_computation.31 | loop fusion | bytes 4194308 | tf_op jit(solution)/shard_map/dynamic_update_slice | solution.py:89
  199.2 7.1 %collective-permute-done.6 = bf16[1024,1024]{1,0:T(8,128)(2,1)} collective-permute-done((bf16[1024,1024]{1,0:T(8,128)(2,1)}, bf16[1024,1024]{1,0:T(8,128)(2,1)}, u32[]{:S(2)}, u32[]{:S(2)}) %collective-permute-start.6) | collective-permute-done | bytes 2097184 | tf_op jit(solution)/shard_map/ppermute | solution.py:83
  206.3 3.3 %constant_dynamic-update-slice_fusion = bf16[8192,1024]{1,0:T(8,128)(2,1)} fusion(bf16[8192,1024]{1,0:T(8,128)(2,1)} %constant_dynamic-update-slice_fusion.1, bf16[1024,1024]{1,0:T(8,128)(2,1)} %collective-permute-done.6, s32[]{:T(128)S(6)} %select_n.82), kind=kLoop, calls=%fused_computation.30 | loop fusion | bytes 4194308 | tf_op jit(solution)/shard_map/dynamic_update_slice | solution.py:84
  209.6 24.6 %fusion.17 = f32[8192,384]{0,1:T(8,128)} fusion(bf16[8192,1024]{1,0:T(8,128)(2,1)} %constant_dynamic-update-slice_fusion, bf16[384,1024]{1,0:T(8,128)(2,1)S(1)} %copy-done), kind=kOutput, calls=%fused_computation.51 | convolution fusion | flops 6442450944 | bytes 30146560 | tf_op jit(solution)/shard_map/dot_general | solution.py:94
  234.2 8.7 %multiply_convert_fusion = bf16[3,128,8192]{2,1,0:T(8,128)(2,1)} fusion(f32[3,128,8192]{2,1,0:T(8,128)} %bitcast.61, f32[3,128,8192]{2,1,0:T(8,128)S(1)} %fusion.2, f32[3,128]{1,0:T(4,128)S(1)} %fusion.13), kind=kLoop, calls=%fused_computation.2 | loop fusion | flops 9437184 | bytes 31458816 | tf_op jit(solution)/shard_map/convert_element_type | solution.py:105
  242.9 10.5 %fusion.19 = f32[1024,384]{0,1:T(8,128)S(1)} fusion(bf16[384,8192]{1,0:T(8,128)(2,1)S(1)} %bitcast.60, bf16[8192,1024]{1,0:T(8,128)(2,1)} %constant_dynamic-update-slice_fusion), kind=kOutput, calls=%fused_computation.53 | convolution fusion | flops 6442450944 | bytes 24641536 | tf_op jit(solution)/shard_map/dot_general | solution.py:93
  253.4 1.1 multiply_convert_fusion.1
  (39 shorter events, 4.0 us)
Async XLA Ops:
  7.2 63.9 %copy-start = (bf16[384,1024]{1,0:T(8,128)(2,1)S(1)}, bf16[384,1024]{1,0:T(8,128)(2,1)}, u32[]{:S(2)}) copy-start(bf16[384,1024]{1,0:T(8,128)(2,1)} %param.9) | copy-start | bytes 2359300
  7.2 138.9 %all-gather.2.cloned.1.call-start = ((), (), s32[]{:S(2)}) async-start(), calls=%async_computation.2 | async-start | bytes 2359296 | tf_op jit(solution)/shard_map/all_gather | solution.py:36
  7.2 70.5 %collective-permute-start = (bf16[1024,1024]{1,0:T(8,128)(2,1)}, bf16[1024,1024]{1,0:T(8,128)(2,1)S(1)}, u32[]{:S(2)}, u32[]{:S(2)}) collective-permute-start(bf16[1024,1024]{1,0:T(8,128)(2,1)} %param.10), channel_id=1, source_target_pairs={{0,4},{4,8},{8,12},{12,16},{16,20},{20,24},{24,28},{28,0},{1,5},{5... | collective-permute-start | bytes 6291464 | tf_op jit(solution)/shard_map/ppermute | solution.py:83
  7.7 70.4 %collective-permute-start.1 = (bf16[1024,1024]{1,0:T(8,128)(2,1)}, bf16[1024,1024]{1,0:T(8,128)(2,1)}, u32[]{:S(2)}, u32[]{:S(2)}) collective-permute-start(bf16[1024,1024]{1,0:T(8,128)(2,1)} %param.10), channel_id=1, source_target_pairs={{0,28},{4,0},{8,4},{12,8},{16,12},{20,16},{24,20},{28,24},{1,29},{... | collective-permute-start | bytes 6291464 | tf_op jit(solution)/shard_map/ppermute | solution.py:88
  10.7 243.8 %reduce-scatter.3.cloned.1.call-start = ((), (), s32[]{:S(2)}) async-start(), calls=%async_computation.3 | async-start | bytes 2359296 | tf_op jit(solution)/shard_map/reduce_scatter | solution.py:122
  77.8 56.2 %collective-permute-start.2 = (bf16[1024,1024]{1,0:T(8,128)(2,1)S(1)}, bf16[1024,1024]{1,0:T(8,128)(2,1)}, u32[]{:S(2)}, u32[]{:S(2)}) collective-permute-start(bf16[1024,1024]{1,0:T(8,128)(2,1)S(1)} %collective-permute-done), channel_id=1, source_target_pairs={{0,4},{4,8},{8,12},{12,16},{16,20},{20,24},{24,28},{28,0},{1,5},{5... | collective-permute-start | bytes 6291464 | tf_op jit(solution)/shard_map/ppermute | solution.py:83
  78.2 71.4 %collective-permute-start.3 = (bf16[1024,1024]{1,0:T(8,128)(2,1)}, bf16[1024,1024]{1,0:T(8,128)(2,1)}, u32[]{:S(2)}, u32[]{:S(2)}) collective-permute-start(bf16[1024,1024]{1,0:T(8,128)(2,1)} %collective-permute-done.1), channel_id=1, source_target_pairs={{0,28},{4,0},{8,4},{12,8},{16,12},{20,16},{24,20},{28,24},{1,29},{... | collective-permute-start | bytes 6291464 | tf_op jit(solution)/shard_map/ppermute | solution.py:88
  82.7 171.9 %reduce-scatter.5.cloned.1.call-start = ((), (), s32[]{:S(2)}) async-start(), calls=%async_computation.4 | async-start | bytes 294912 | tf_op jit(solution)/shard_map/reduce_scatter | solution.py:128
  133.9 36.1 %collective-permute-start.4 = (bf16[1024,1024]{1,0:T(8,128)(2,1)}, bf16[1024,1024]{1,0:T(8,128)(2,1)}, u32[]{:S(2)}, u32[]{:S(2)}) collective-permute-start(bf16[1024,1024]{1,0:T(8,128)(2,1)} %collective-permute-done.2), channel_id=1, source_target_pairs={{0,4},{4,8},{8,12},{12,16},{16,20},{20,24},{24,28},{28,0},{1,5},{5... | collective-permute-start | bytes 6291464 | tf_op jit(solution)/shard_map/ppermute | solution.py:83
  133.9 6.0 %copy-start.2 = (bf16[1024,1024]{1,0:T(8,128)(2,1)S(1)}, bf16[1024,1024]{1,0:T(8,128)(2,1)}, u32[]{:S(2)}) copy-start(bf16[1024,1024]{1,0:T(8,128)(2,1)} %param.10) | copy-start | bytes 6291460
  133.9 7.5 %copy-start.3 = (s32[3]{0:T(128)S(1)}, s32[3]{0:T(128)}, u32[]{:S(2)}) copy-start(s32[3]{0:T(128)} %param.14) | copy-start | bytes 40
  149.6 46.5 %collective-permute-start.5 = (bf16[1024,1024]{1,0:T(8,128)(2,1)}, bf16[1024,1024]{1,0:T(8,128)(2,1)}, u32[]{:S(2)}, u32[]{:S(2)}) collective-permute-start(bf16[1024,1024]{1,0:T(8,128)(2,1)} %collective-permute-done.3), channel_id=1, source_target_pairs={{0,28},{4,0},{8,4},{12,8},{16,12},{20,16},{24,20},{28,24},{1,29},{... | collective-permute-start | bytes 6291464 | tf_op jit(solution)/shard_map/ppermute | solution.py:88
  170.0 36.3 %collective-permute-start.6 = (bf16[1024,1024]{1,0:T(8,128)(2,1)}, bf16[1024,1024]{1,0:T(8,128)(2,1)}, u32[]{:S(2)}, u32[]{:S(2)}) collective-permute-start(bf16[1024,1024]{1,0:T(8,128)(2,1)} %collective-permute-done.4), channel_id=1, source_target_pairs={{0,4},{4,8},{8,12},{12,16},{16,20},{20,24},{24,28},{28,0},{1,5},{5... | collective-permute-start | bytes 6291464 | tf_op jit(solution)/shard_map/ppermute | solution.py:83
  206.3 36.6 %slice-start = ((s8[6291456]{0:T(1024)(128)(4,1)}), s8[4194304]{0:T(1024)(128)(4,1)S(1)}, s32[]{:S(2)}) async-start(s8[6291456]{0:T(1024)(128)(4,1)} %bitcast.59), calls=%async_computation.5 | async-start | bytes 8388608
  209.6 33.3 %slice-start.1 = ((s8[6291456]{0:T(1024)(128)(4,1)}), s8[2097152]{0:T(1024)(128)(4,1)S(1)}, s32[]{:S(2)}) async-start(s8[6291456]{0:T(1024)(128)(4,1)} %bitcast.59), calls=%async_computation.6 | async-start | bytes 4194304
  242.9 11.7 %copy-start.1 = (bf16[384,1024]{1,0:T(8,128)(2,1)S(1)}, bf16[384,1024]{1,0:T(8,128)(2,1)}, u32[]{:S(2)}) copy-start(bf16[384,1024]{1,0:T(8,128)(2,1)} %param.9) | copy-start | bytes 2359300
Sparse Core Ops, SparseCore 0:
  10.8 38.1 all-gather.1
  82.8 50.4 reduce-scatter.2
  172.0 35.8 reduce-scatter.4
